TPU v7x, 128 devices: a whole 4x4x4 slice. The times are simulated.
128 devices in a mesh: leaf: 16 (over z, x), panel: 8 (over y, core).
Axes of the slice: x: 4, y: 4, z: 4, core: 2. Of those that a mesh axis runs over, the one named last changes fastest.
Arguments:
- child_front: float32 [16, 2048, 2048], P('leaf', 'panel'), as said below
- child_panel: bfloat16 [16, 2048, 4096], P('leaf'), may hold values from -0.03125 to 0.03125
- parent_front: float32 [4096, 4096], P('leaf', 'panel'), as said below
- tile_map: int32 [16, 8], P('leaf'), may hold values from 0 to 15, as said below
- tile_count: int32 [16], P('leaf'), may hold values from 2 to 8, as said below
Outputs:
- eliminated: float32 [4096, 4096], P('leaf', 'panel')
Inputs may be any that keep to these rules, and one draw needn't show every extreme that they name: `tile_count`: some child has 8 live tiles and some child has 2. `tile_map`: for child c the first tile_count[c] entries are distinct and rising; the other entries are 0. Each child's block is symmetric, and child_front[c] - child_panel[c] child_panel[c]^T is positive definite. `parent_front`: symmetric positive definite.
All inputs are finite; a program needn't handle non-finite values.
Results may differ from a plain program's by a relative error of at most 0.0003.
Values sent between devices are 32-bit elements; how exact they have to be, the bound alone decides.
No kernel may reach another device: no remote copies, remote signals or barrier semaphores. Data moves between devices by JAX's collectives and lax.ppermute only.
A program may use at most 128 MiB of HBM per device.

v0:
```python
import jax
import jax.numpy as jnp
from jax import lax
from jax.sharding import PartitionSpec as P

TILE = 256
NF = 4096
CB = 2048
STEPS = 4


def spread(array, axis, root):
    mine = lax.axis_index(axis) == root
    return lax.psum(jnp.where(mine, array, jnp.zeros_like(array)), axis)


def finish_rows(block, row_index, factor, pivot_start):
    solved = lax.linalg.triangular_solve(
        factor, block, left_side=False, lower=True, transpose_a=True
    )
    offset = jnp.clip(row_index - pivot_start, 0, TILE - 1)
    own_rows = jnp.take(factor, offset, axis=0)
    inside = (row_index >= pivot_start) & (row_index < pivot_start + TILE)
    kept = jnp.where(inside[:, None], own_rows, solved)
    return jnp.where(row_index[:, None] < pivot_start, 0.0, kept)


def shards(child_front, child_panel, parent_front, tile_map, tile_count):
    highest = lax.Precision.HIGHEST
    panel_count = lax.axis_size("panel")
    leaf_id = lax.axis_index("leaf")
    panel_id = lax.axis_index("panel")
    tiles_child = CB // TILE
    tiles_front = NF // TILE
    pivot_span = STEPS * TILE
    child_rows = child_front.shape[1]
    height = parent_front.shape[0]
    col_width = parent_front.shape[1]
    panel_all = child_panel[0]
    own_panel = lax.dynamic_slice_in_dim(panel_all, panel_id * child_rows, child_rows, 0)
    update = child_front[0] - lax.dot_general(
        own_panel, panel_all, (((1,), (1,)), ((), ())), preferred_element_type=jnp.float32
    )
    mapped = tile_map[0]
    live_tiles = jnp.arange(tiles_child, dtype=jnp.int32) < tile_count[0]
    everywhere = jnp.arange(tiles_front, dtype=jnp.int32)
    chosen = ((mapped[None, :] == everywhere[:, None]) & live_tiles[None, :]).astype(jnp.float32)
    placed = jnp.einsum(
        "rtb,ft->rfb", update.reshape(child_rows, tiles_child, TILE), chosen, precision=highest
    )
    placed = placed.reshape(child_rows, panel_count, col_width)
    moved_cols = lax.all_to_all(placed, "panel", split_axis=1, concat_axis=0, tiled=True)
    column_tiles = moved_cols.reshape(tiles_child, TILE, col_width)
    targets = jnp.arange(lax.axis_size("leaf") * height // TILE, dtype=jnp.int32)
    picked = ((mapped[None, :] == targets[:, None]) & live_tiles[None, :]).astype(jnp.float32)
    front_block = parent_front + lax.psum_scatter(
        jnp.einsum("ft,tbc->fbc", picked, column_tiles, precision=highest).reshape(
            lax.axis_size("leaf") * height, col_width
        ),
        "leaf",
        scatter_dimension=0,
        tiled=True,
    )
    global_rows = leaf_id * height + jnp.arange(height, dtype=jnp.int32)
    global_cols = panel_id * col_width + jnp.arange(col_width, dtype=jnp.int32)
    col_tiles = col_width // TILE
    for pivot_step in range(STEPS):
        source_panel = pivot_step // col_tiles
        local_start = pivot_step % col_tiles * TILE
        pivot_start = pivot_step * TILE
        source = front_block[:, local_start : local_start + TILE]
        column = spread(source, "panel", source_panel)
        full_column = lax.all_gather(column, "leaf", axis=0, tiled=True)
        factor = jnp.linalg.cholesky(full_column[pivot_start : pivot_start + TILE])
        own_factor = finish_rows(column, global_rows, factor, pivot_start)
        col_factor = finish_rows(
            lax.dynamic_slice_in_dim(full_column, panel_id * col_width, col_width, 0),
            global_cols,
            factor,
            pivot_start,
        )
        front_block = front_block - lax.dot_general(
            own_factor,
            col_factor,
            (((1,), (1,)), ((), ())),
            precision=highest,
            preferred_element_type=jnp.float32,
        )
        replaced = jnp.where(
            panel_id == source_panel, own_factor, front_block[:, local_start : local_start + TILE]
        )
        front_block = front_block.at[:, local_start : local_start + TILE].set(replaced)
    upper_zone = (global_rows[:, None] < pivot_span) & (global_cols[None, :] >= pivot_span)
    return jnp.where(upper_zone, 0.0, front_block)


def solution(mesh):
    placed = (
        P("leaf", "panel", None),
        P("leaf", None, None),
        P("leaf", "panel"),
        P("leaf", None),
        P("leaf"),
    )
    return jax.shard_map(
        shards, mesh=mesh, in_specs=placed, out_specs=P("leaf", "panel"), check_vma=False
    )
```

profile of v0, /device:TPU:0, one launch (start us, length us, event | category | flops | bytes accessed | tf_op | source)
XLA Modules:
  0.0 964.4 jit_solution(7068307118465232745)
XLA Ops:
  6.5 11.5 %fusion.2 = f32[256,2048]{1,0:T(8,128)S(1)} fusion(bf16[1,2048,4096]{2,1,0:T(8,128)(2,1)} %param.23, f32[1,256,2048]{2,1,0:T(8,128)} %param.22, s32[]{:T(128)S(6)} %select_n.120), kind=kOutput, calls=%fused_computation.18 | convolution fusion | flops 4295491584 | bytes 23068676 | tf_op jit(solution)/shard_map/dot_general | solution.py:41
  23.2 5.2 reshape.226
  33.0 54.3 %all_to_all.15 = f32[256,8,512]{2,0,1:T(8,128)} all-to-all(f32[256,8,512]{2,0,1:T(8,128)S(1)} %copy.25), channel_id=1, replica_groups=mesh['leaf'=16,'panel'=8] {'panel'}, dimensions={1} | all-to-all | bytes 8388608 | tf_op jit(solution)/shard_map/all_to_all | solution.py:52
  87.4 5.5 copy.46
  92.8 5.5 fusion.118
  98.4 11.3 %copy.54 = f32[64,8,16,256]{3,1,2,0:T(8,128)} copy(f32[64,8,16,256]{3,2,1,0:T(8,128)S(1)} %bitcast.200) | data formatting | bytes 16777216
  110.9 85.6 %reduce-scatter.2.cloned.1.call-done = f32[256,512]{0,1:T(8,128)} async-done(((f32[4096,512]{0,1:T(8,128)}), f32[256,512]{0,1:T(8,128)}) %reduce-scatter.2.cloned.1.call-update) | async-done | bytes 524304 | tf_op jit(solution)/shard_map/reduce_scatter | solution.py:56
  198.4 60.0 %all-reduce.6.cloned.1.call-done = f32[256,256]{0,1:T(8,128)} async-done(((f32[256,256]{0,1:T(8,128)}), f32[256,256]{0,1:T(8,128)}) %all-reduce.6.cloned.1.call-update) | async-done | bytes 262160 | tf_op jit(solution)/shard_map/psum | solution.py:14
  259.5 57.1 %all-gather.5.cloned.1.call-done = f32[4096,256]{0,1:T(8,128)} async-done(((f32[256,256]{0,1:T(8,128)}), f32[4096,256]{0,1:T(8,128)}) %all-gather.5.cloned.1.call-update) | async-done | bytes 4194320 | tf_op jit(solution)/shard_map/all_gather | solution.py:73
  318.7 11.7 %cholesky.214 = f32[128,128]{1,0:T(8,128)S(1)} custom-call(f32[128,128]{1,0:T(8,128)S(1)} %cholesky.346), custom_call_target="Cholesky" | custom-call | tf_op jit(solution)/shard_map/jit(cholesky)/cholesky | solution.py:74
  330.4 9.8 %custom-call.23 = f32[1,128,128]{1,2,0:T(8,128)S(1)} custom-call(f32[1,128,128]{2,1,0:T(8,128)S(1)} %get-tuple-element.181), custom_call_target="InvertDiagBlocksLowerTriangular" | custom-call | tf_op jit(solution)/shard_map/jit(cholesky)/cholesky | solution.py:74
  340.7 11.7 %cholesky.231 = f32[128,128]{1,0:T(8,128)S(1)} custom-call(f32[128,128]{1,0:T(8,128)S(1)} %convolution_subtract_fusion.15), custom_call_target="Cholesky" | custom-call | tf_op jit(solution)/shard_map/jit(cholesky)/cholesky | solution.py:74
  358.8 20.1 %custom-call.24 = f32[2,128,128]{1,2,0:T(8,128)S(1)} custom-call(f32[2,128,128]{2,1,0:T(8,128)S(1)} %get-tuple-element.110), custom_call_target="InvertDiagBlocksLowerTriangular" | custom-call | tf_op jit(solution)/shard_map/triangular_solve/custom-call.0 | solution.py:18
  388.4 59.7 %all-reduce.8.cloned.1.call-done = f32[256,256]{0,1:T(8,128)} async-done(((f32[256,256]{0,1:T(8,128)}), f32[256,256]{0,1:T(8,128)}) %all-reduce.8.cloned.1.call-update) | async-done | bytes 262160 | tf_op jit(solution)/shard_map/psum | solution.py:14
  448.5 57.6 %all-gather.7.cloned.1.call-done = f32[4096,256]{0,1:T(8,128)} async-done(((f32[256,256]{0,1:T(8,128)}), f32[4096,256]{0,1:T(8,128)}) %all-gather.7.cloned.1.call-update) | async-done | bytes 4194320 | tf_op jit(solution)/shard_map/all_gather | solution.py:73
  508.3 11.7 %cholesky.248 = f32[128,128]{1,0:T(8,128)S(1)} custom-call(f32[128,128]{1,0:T(8,128)S(1)} %cholesky.349), custom_call_target="Cholesky" | custom-call | tf_op jit(solution)/shard_map/jit(cholesky)/cholesky | solution.py:74
  520.1 9.8 %custom-call.26 = f32[1,128,128]{1,2,0:T(8,128)S(1)} custom-call(f32[1,128,128]{2,1,0:T(8,128)S(1)} %get-tuple-element.177), custom_call_target="InvertDiagBlocksLowerTriangular" | custom-call | tf_op jit(solution)/shard_map/jit(cholesky)/cholesky | solution.py:74
  530.3 11.7 %cholesky.265 = f32[128,128]{1,0:T(8,128)S(1)} custom-call(f32[128,128]{1,0:T(8,128)S(1)} %convolution_subtract_fusion.14), custom_call_target="Cholesky" | custom-call | tf_op jit(solution)/shard_map/jit(cholesky)/cholesky | solution.py:74
  549.3 19.7 %custom-call.27 = f32[2,128,128]{1,2,0:T(8,128)S(1)} custom-call(f32[2,128,128]{2,1,0:T(8,128)S(1)} %get-tuple-element.112), custom_call_target="InvertDiagBlocksLowerTriangular" | custom-call | tf_op jit(solution)/shard_map/triangular_solve/custom-call.0 | solution.py:18
  577.8 59.7 %all-reduce.10.cloned.1.call-done = f32[256,256]{0,1:T(8,128)} async-done(((f32[256,256]{0,1:T(8,128)}), f32[256,256]{0,1:T(8,128)}) %all-reduce.10.cloned.1.call-update) | async-done | bytes 262160 | tf_op jit(solution)/shard_map/psum | solution.py:14
  637.9 57.7 %all-gather.9.cloned.1.call-done = f32[4096,256]{0,1:T(8,128)} async-done(((f32[256,256]{0,1:T(8,128)}), f32[4096,256]{0,1:T(8,128)}) %all-gather.9.cloned.1.call-update) | async-done | bytes 4194320 | tf_op jit(solution)/shard_map/all_gather | solution.py:73
  697.7 11.7 %cholesky.282 = f32[128,128]{1,0:T(8,128)S(1)} custom-call(f32[128,128]{1,0:T(8,128)S(1)} %cholesky.352), custom_call_target="Cholesky" | custom-call | tf_op jit(solution)/shard_map/jit(cholesky)/cholesky | solution.py:74
  709.5 9.8 %custom-call.29 = f32[1,128,128]{1,2,0:T(8,128)S(1)} custom-call(f32[1,128,128]{2,1,0:T(8,128)S(1)} %get-tuple-element.173), custom_call_target="InvertDiagBlocksLowerTriangular" | custom-call | tf_op jit(solution)/shard_map/jit(cholesky)/cholesky | solution.py:74
  719.8 11.7 %cholesky.299 = f32[128,128]{1,0:T(8,128)S(1)} custom-call(f32[128,128]{1,0:T(8,128)S(1)} %convolution_subtract_fusion.13), custom_call_target="Cholesky" | custom-call | tf_op jit(solution)/shard_map/jit(cholesky)/cholesky | solution.py:74
  734.3 4.6 while.22
  739.0 19.7 %custom-call.30 = f32[2,128,128]{1,2,0:T(8,128)S(1)} custom-call(f32[2,128,128]{2,1,0:T(8,128)S(1)} %get-tuple-element.114), custom_call_target="InvertDiagBlocksLowerTriangular" | custom-call | tf_op jit(solution)/shard_map/triangular_solve/custom-call.0 | solution.py:18
  768.4 59.5 %all-reduce.12.cloned.1.call-done = f32[256,256]{0,1:T(8,128)} async-done(((f32[256,256]{0,1:T(8,128)}), f32[256,256]{0,1:T(8,128)}) %all-reduce.12.cloned.1.call-update) | async-done | bytes 262160 | tf_op jit(solution)/shard_map/psum | solution.py:14
  828.0 58.0 %all-gather.11.cloned.1.call-done = f32[4096,256]{0,1:T(8,128)} async-done(((f32[256,256]{0,1:T(8,128)}), f32[4096,256]{0,1:T(8,128)}) %all-gather.11.cloned.1.call-update) | async-done | bytes 4194320 | tf_op jit(solution)/shard_map/all_gather | solution.py:73
  888.1 11.7 %cholesky.316 = f32[128,128]{1,0:T(8,128)S(1)} custom-call(f32[128,128]{1,0:T(8,128)S(1)} %cholesky.355), custom_call_target="Cholesky" | custom-call | tf_op jit(solution)/shard_map/jit(cholesky)/cholesky | solution.py:74
  899.9 9.8 %custom-call.32 = f32[1,128,128]{1,2,0:T(8,128)S(1)} custom-call(f32[1,128,128]{2,1,0:T(8,128)S(1)} %get-tuple-element.169), custom_call_target="InvertDiagBlocksLowerTriangular" | custom-call | tf_op jit(solution)/shard_map/jit(cholesky)/cholesky | solution.py:74
  910.2 11.7 %cholesky.333 = f32[128,128]{1,0:T(8,128)S(1)} custom-call(f32[128,128]{1,0:T(8,128)S(1)} %convolution_subtract_fusion.12), custom_call_target="Cholesky" | custom-call | tf_op jit(solution)/shard_map/jit(cholesky)/cholesky | solution.py:74
  928.8 19.7 %custom-call.33 = f32[2,128,128]{1,2,0:T(8,128)S(1)} custom-call(f32[2,128,128]{2,1,0:T(8,128)S(1)} %get-tuple-element.116), custom_call_target="InvertDiagBlocksLowerTriangular" | custom-call | tf_op jit(solution)/shard_map/triangular_solve/custom-call.0 | solution.py:18
  (202 shorter events, 95.5 us)
Async XLA Ops:
  6.5 190.0 %reduce-scatter.2.cloned.1.call-start = ((), (), s32[]{:S(2)}) async-start(), calls=%async_computation.2 | async-start | bytes 8912896 | tf_op jit(solution)/shard_map/reduce_scatter | solution.py:56
  18.0 1.6 copy-start.5
  109.7 1.0 copy-start.4
  109.7 148.7 %all-reduce.6.cloned.1.call-start = ((), (), s32[]{:S(2)}) async-start(), calls=%async_computation.3 | async-start | bytes 524288 | tf_op jit(solution)/shard_map/psum | solution.py:14
  198.3 118.2 %all-gather.5.cloned.1.call-start = ((), (), s32[]{:S(2)}) async-start(), calls=%async_computation.4 | async-start | bytes 4456448 | tf_op jit(solution)/shard_map/all_gather | solution.py:73
  258.4 120.5 %copy-start = (f32[256,256]{0,1:T(8,128)S(1)}, f32[256,256]{0,1:T(8,128)}, u32[]{:S(2)}) copy-start(f32[256,256]{0,1:T(8,128)} %all-reduce.6.cloned.1.call-done) | copy-start | bytes 786436
  258.4 189.7 %all-reduce.8.cloned.1.call-start = ((), (), s32[]{:S(2)}) async-start(), calls=%async_computation.5 | async-start | bytes 524288 | tf_op jit(solution)/shard_map/psum | solution.py:14
  388.4 117.8 %all-gather.7.cloned.1.call-start = ((), (), s32[]{:S(2)}) async-start(), calls=%async_computation.6 | async-start | bytes 4456448 | tf_op jit(solution)/shard_map/all_gather | solution.py:73
  448.2 120.8 %copy-start.2 = (f32[256,256]{0,1:T(8,128)S(1)}, f32[256,256]{0,1:T(8,128)}, u32[]{:S(2)}) copy-start(f32[256,256]{0,1:T(8,128)} %all-reduce.8.cloned.1.call-done) | copy-start | bytes 786436
  448.2 189.3 %all-reduce.10.cloned.1.call-start = ((), (), s32[]{:S(2)}) async-start(), calls=%async_computation.7 | async-start | bytes 524288 | tf_op jit(solution)/shard_map/psum | solution.py:14
  577.8 117.9 %all-gather.9.cloned.1.call-start = ((), (), s32[]{:S(2)}) async-start(), calls=%async_computation.8 | async-start | bytes 4456448 | tf_op jit(solution)/shard_map/all_gather | solution.py:73
  637.5 121.2 %copy-start.3 = (f32[256,256]{0,1:T(8,128)S(1)}, f32[256,256]{0,1:T(8,128)}, u32[]{:S(2)}) copy-start(f32[256,256]{0,1:T(8,128)} %all-reduce.10.cloned.1.call-done) | copy-start | bytes 786436
  637.5 190.3 %all-reduce.12.cloned.1.call-start = ((), (), s32[]{:S(2)}) async-start(), calls=%async_computation.9 | async-start | bytes 524288 | tf_op jit(solution)/shard_map/psum | solution.py:14
  768.1 117.9 %all-gather.11.cloned.1.call-start = ((), (), s32[]{:S(2)}) async-start(), calls=%async_computation.10 | async-start | bytes 4456448 | tf_op jit(solution)/shard_map/all_gather | solution.py:73
  827.8 120.6 %copy-start.1 = (f32[256,256]{0,1:T(8,128)S(1)}, f32[256,256]{0,1:T(8,128)}, u32[]{:S(2)}) copy-start(f32[256,256]{0,1:T(8,128)} %all-reduce.12.cloned.1.call-done) | copy-start | bytes 786436
Sparse Core Ops, SparseCore 0:
  109.8 86.6 reduce-scatter.1
  198.8 59.5 all-reduce.5
  260.5 55.9 all-gather.4
  388.5 59.6 all-reduce.7
  450.1 55.9 all-gather.6
  577.9 59.5 all-reduce.9
  639.6 55.9 all-gather.8
  768.3 59.5 all-reduce.11
  830.0 55.9 all-gather.10
where the time goes:
time: 972 us; the launch traced here: 964 us
  waiting for transfers between devices  555 us (57%)
  other arithmetic  228 us (23%)
  local copies, waits for them, and re-layouts  62 us (6%)
  blocking collectives  54.3 us (6%)
  matrix products  42.7 us (4%)
  between operations  20.3 us (2%)
    psum x4, waiting for transfers between devices, spread(): return lax.psum(jnp.where(mine, array, jnp.zeros_like(array)), axis)  239 us
    all_gather x4, waiting for transfers between devices, shards(): full_column = lax.all_gather(column, 'leaf', axis=0, tiled=True)  230 us
    another operation x27, other arithmetic, shards(): factor = jnp.linalg.cholesky(full_column[pivot_start:pivot_start + TILE])  138 us
    reduce_scatter x1, waiting for transfers between devices, shards(): lax.psum_scatter(jnp.einsum('ft,tbc->fbc', picked, column_tiles, precisio...  85.6 us
    another operation x9, other arithmetic, finish_rows(): lax.linalg.triangular_solve(factor, block, left_side=False, lower=True, t...  79.3 us
    all_to_all x1, blocking collectives, shards(): lax.all_to_all(placed, 'panel', split_axis=1, concat_axis=0, tiled=True)  54.3 us
  transfers between devices with their start and end apart: 9, of which 9 were waited for; matrix products, arithmetic and copies ran while one was open for 0% of the time, Pallas kernels for 0%

commit v1 on v0

--- a/solution.py
+++ b/solution.py
@@ -7,6 +7,14 @@
 NF = 4096
 CB = 2048
 STEPS = 4
+
+
+def switch_sector_here(array_in, axis_k):
+    array_in = jnp.moveaxis(array_in, 0, axis_k)
+    arr_next = array_in.shape
+    return array_in.reshape(
+        *arr_next[:axis_k], arr_next[axis_k] * arr_next[axis_k + 1], *arr_next[axis_k + 2 :]
+    )
 
 
 def spread(array, axis, root):
@@ -70,7 +78,23 @@
         pivot_start = pivot_step * TILE
         source = front_block[:, local_start : local_start + TILE]
         column = spread(source, "panel", source_panel)
-        full_column = lax.all_gather(column, "leaf", axis=0, tiled=True)
+        degree = jax.lax.axis_size("leaf")
+        all_rows = [(b, (b + 1) % degree) for b in range(degree)]
+        piece_out, even = ([], [])
+        blocks_here = [(q, w) for w, q in all_rows]
+        for ii in range(degree - 1):
+            if ii % 2 == 0:
+                o_now = jax.lax.ppermute(piece_out[-1] if piece_out else column, "leaf", all_rows)
+                piece_out.append(o_now)
+            else:
+                mid_arr = jax.lax.ppermute(even[-1] if even else column, "leaf", blocks_here)
+                even.append(mid_arr)
+        raw_out = jnp.stack([*piece_out[::-1], column, *even], axis=0)
+        a_now = len(piece_out)
+        far_arr = jax.lax.axis_index("leaf")
+        work_now = far_arr - a_now
+        raw_out = raw_out[(jnp.arange(degree) - work_now) % degree]
+        full_column = switch_sector_here(raw_out, 0)
         factor = jnp.linalg.cholesky(full_column[pivot_start : pivot_start + TILE])
         own_factor = finish_rows(column, global_rows, factor, pivot_start)
         col_factor = finish_rows(

time: 972 us -> 1160 us (1.19)
  starting transfers between devices: 1.13 us -> 164 us
  local copies, waits for them, and re-layouts: 62 us -> 162 us
  waiting for transfers between devices: 555 us -> 482 us
    all_gather x4 -> x0, waiting for transfers between devices: 230 us -> none  [shards(): full_column = lax.all_gather(column, 'leaf', axis=0, tiled=True)]
    ppermute x0 -> x60, waiting for transfers between devices: none -> 175 us  [the longest x32 173 us: shards(): jax.lax.ppermute(piece_out[-1] if piece_out else column, 'leaf', all_rows)]
    ppermute x0 -> x60, starting transfers between devices: none -> 164 us  [the longest x28 158 us: shards(): jax.lax.ppermute(even[-1] if even else column, 'leaf', blocks_here)]
    unnamed x15 -> x78, local copies, waits for them, and re-layouts: 13.4 us -> 57.7 us
    gather x0 -> x8, local copies, waits for them, and re-layouts: none -> 41.5 us  [shards(): raw_out = raw_out[(jnp.arange(degree) - work_now) % degree]]
    psum x4, waiting for transfers between devices: 239 us -> 222 us  [spread(): return lax.psum(jnp.where(mine, array, jnp.zeros_like(array)), axis)]
  transfers between devices with their start and end apart: 9 -> 65, of which waited for: 9 -> 46; matrix products, arithmetic and copies ran while one was open for 0% -> 5% of each run, Pallas kernels for 0% -> 0%
where the time goes in v1:
time: 1160 us; the launch traced here: 1150 us
  waiting for transfers between devices  482 us (42%)
  other arithmetic  228 us (20%)
  starting transfers between devices  164 us (14%)
  local copies, waits for them, and re-layouts  162 us (14%)
  blocking collectives  54.2 us (5%)
  matrix products  43.8 us (4%)
  between operations  20.1 us (2%)
    psum x4, waiting for transfers between devices, spread(): return lax.psum(jnp.where(mine, array, jnp.zeros_like(array)), axis)  222 us
    ppermute x32, waiting for transfers between devices, shards(): jax.lax.ppermute(piece_out[-1] if piece_out else column, 'leaf', all_rows)  173 us
    ppermute x28, starting transfers between devices, shards(): jax.lax.ppermute(even[-1] if even else column, 'leaf', blocks_here)  158 us
    another operation x27, other arithmetic, shards(): factor = jnp.linalg.cholesky(full_column[pivot_start:pivot_start + TILE])  138 us
    reduce_scatter x1, waiting for transfers between devices, shards(): lax.psum_scatter(jnp.einsum('ft,tbc->fbc', picked, column_tiles, precisio...  85.3 us
    another operation x9, other arithmetic, finish_rows(): lax.linalg.triangular_solve(factor, block, left_side=False, lower=True, t...  79.8 us
    unnamed x78, local copies, waits for them, and re-layouts  57.7 us
    all_to_all x1, blocking collectives, shards(): lax.all_to_all(placed, 'panel', split_axis=1, concat_axis=0, tiled=True)  54.2 us
  transfers between devices with their start and end apart: 65, of which 46 were waited for; matrix products, arithmetic and copies ran while one was open for 5% of the time, Pallas kernels for 0%

profile of v1, /device:TPU:0, one launch (start us, length us, event | category | flops | bytes accessed | tf_op | source)
XLA Modules:
  0.0 1154.6 jit_solution(13844293767801567548)
XLA Ops:
  6.5 11.5 fusion.5
  33.1 54.2 %all_to_all.15 = f32[256,8,512]{2,0,1:T(8,128)S(1)} all-to-all(f32[256,8,512]{2,0,1:T(8,128)S(1)} %copy.48), channel_id=1, replica_groups=mesh['leaf'=16,'panel'=8] {'panel'}, dimensions={1} | all-to-all | bytes 8388608 | tf_op jit(solution)/shard_map/all_to_all | solution.py:60
  93.1 8.1 copy.50
  101.2 8.9 copy.51
  111.4 85.3 %reduce-scatter.2.cloned.1.call-done = f32[256,512]{0,1:T(8,128)} async-done(((f32[4096,512]{0,1:T(8,128)}), f32[256,512]{0,1:T(8,128)}) %reduce-scatter.2.cloned.1.call-update) | async-done | bytes 524304 | tf_op jit(solution)/shard_map/reduce_scatter | solution.py:64
  198.6 60.1 %all-reduce.6.cloned.1.call-done = f32[256,256]{0,1:T(8,128)} async-done(((f32[256,256]{0,1:T(8,128)}), f32[256,256]{0,1:T(8,128)}) %all-reduce.6.cloned.1.call-update) | async-done | bytes 262160 | tf_op jit(solution)/shard_map/psum | solution.py:22
  260.1 8.4 collective-permute-done
  316.5 6.3 collective-permute-done.5
  328.3 6.4 collective-permute-done.6
  372.5 11.7 %cholesky.214 = f32[128,128]{1,0:T(8,128)S(1)} custom-call(f32[128,128]{1,0:T(8,128)S(1)} %cholesky.346), custom_call_target="Cholesky" | custom-call | tf_op jit(solution)/shard_map/jit(cholesky)/cholesky | solution.py:98
  384.3 9.8 custom-call.23
  394.6 11.7 %cholesky.231 = f32[128,128]{1,0:T(8,128)S(1)} custom-call(f32[128,128]{1,0:T(8,128)S(1)} %convolution_subtract_fusion.15), custom_call_target="Cholesky" | custom-call | tf_op jit(solution)/shard_map/jit(cholesky)/cholesky | solution.py:98
  412.5 19.8 %custom-call.24 = f32[2,128,128]{1,2,0:T(8,128)S(1)} custom-call(f32[2,128,128]{2,1,0:T(8,128)S(1)} %get-tuple-element.110), custom_call_target="InvertDiagBlocksLowerTriangular" | custom-call | tf_op jit(solution)/shard_map/triangular_solve/custom-call.0 | solution.py:26
  442.1 53.8 %all-reduce.8.cloned.1.call-done = f32[256,256]{0,1:T(8,128)} async-done(((f32[256,256]{0,1:T(8,128)}), f32[256,256]{0,1:T(8,128)}) %all-reduce.8.cloned.1.call-update) | async-done | bytes 262160 | tf_op jit(solution)/shard_map/psum | solution.py:22
  497.4 8.4 collective-permute-done.15
  609.0 11.7 %cholesky.248 = f32[128,128]{1,0:T(8,128)S(1)} custom-call(f32[128,128]{1,0:T(8,128)S(1)} %cholesky.349), custom_call_target="Cholesky" | custom-call | tf_op jit(solution)/shard_map/jit(cholesky)/cholesky | solution.py:98
  620.8 9.8 custom-call.26
  631.1 11.7 %cholesky.265 = f32[128,128]{1,0:T(8,128)S(1)} custom-call(f32[128,128]{1,0:T(8,128)S(1)} %convolution_subtract_fusion.14), custom_call_target="Cholesky" | custom-call | tf_op jit(solution)/shard_map/jit(cholesky)/cholesky | solution.py:98
  649.5 20.1 %custom-call.27 = f32[2,128,128]{1,2,0:T(8,128)S(1)} custom-call(f32[2,128,128]{2,1,0:T(8,128)S(1)} %get-tuple-element.112), custom_call_target="InvertDiagBlocksLowerTriangular" | custom-call | tf_op jit(solution)/shard_map/triangular_solve/custom-call.0 | solution.py:26
  678.6 53.8 %all-reduce.10.cloned.1.call-done = f32[256,256]{0,1:T(8,128)} async-done(((f32[256,256]{0,1:T(8,128)}), f32[256,256]{0,1:T(8,128)}) %all-reduce.10.cloned.1.call-update) | async-done | bytes 262160 | tf_op jit(solution)/shard_map/psum | solution.py:22
  733.9 8.4 collective-permute-done.30
  845.6 11.7 %cholesky.282 = f32[128,128]{1,0:T(8,128)S(1)} custom-call(f32[128,128]{1,0:T(8,128)S(1)} %cholesky.352), custom_call_target="Cholesky" | custom-call | tf_op jit(solution)/shard_map/jit(cholesky)/cholesky | solution.py:98
  857.3 9.8 custom-call.29
  867.6 11.7 %cholesky.299 = f32[128,128]{1,0:T(8,128)S(1)} custom-call(f32[128,128]{1,0:T(8,128)S(1)} %convolution_subtract_fusion.13), custom_call_target="Cholesky" | custom-call | tf_op jit(solution)/shard_map/jit(cholesky)/cholesky | solution.py:98
  886.0 19.9 %custom-call.30 = f32[2,128,128]{1,2,0:T(8,128)S(1)} custom-call(f32[2,128,128]{2,1,0:T(8,128)S(1)} %get-tuple-element.114), custom_call_target="InvertDiagBlocksLowerTriangular" | custom-call | tf_op jit(solution)/shard_map/triangular_solve/custom-call.0 | solution.py:26
  915.6 53.9 %all-reduce.12.cloned.1.call-done = f32[256,256]{0,1:T(8,128)} async-done(((f32[256,256]{0,1:T(8,128)}), f32[256,256]{0,1:T(8,128)}) %all-reduce.12.cloned.1.call-update) | async-done | bytes 262160 | tf_op jit(solution)/shard_map/psum | solution.py:22
  971.0 8.4 collective-permute-done.45
  1044.7 6.2 collective-permute-start.59
  1078.2 11.7 %cholesky.316 = f32[128,128]{1,0:T(8,128)S(1)} custom-call(f32[128,128]{1,0:T(8,128)S(1)} %cholesky.355), custom_call_target="Cholesky" | custom-call | tf_op jit(solution)/shard_map/jit(cholesky)/cholesky | solution.py:98
  1090.0 9.8 custom-call.32
  1100.2 11.7 %cholesky.333 = f32[128,128]{1,0:T(8,128)S(1)} custom-call(f32[128,128]{1,0:T(8,128)S(1)} %convolution_subtract_fusion.12), custom_call_target="Cholesky" | custom-call | tf_op jit(solution)/shard_map/jit(cholesky)/cholesky | solution.py:98
  1118.6 19.8 %custom-call.33 = f32[2,128,128]{1,2,0:T(8,128)S(1)} custom-call(f32[2,128,128]{2,1,0:T(8,128)S(1)} %get-tuple-element.116), custom_call_target="InvertDiagBlocksLowerTriangular" | custom-call | tf_op jit(solution)/shard_map/triangular_solve/custom-call.0 | solution.py:26
  (388 shorter events, 495.3 us)
Async XLA Ops:
  6.5 190.1 %reduce-scatter.2.cloned.1.call-start = ((), (), s32[]{:S(2)}) async-start(), calls=%async_computation.2 | async-start | bytes 8912896 | tf_op jit(solution)/shard_map/reduce_scatter | solution.py:64
  110.2 148.5 %all-reduce.6.cloned.1.call-start = ((), (), s32[]{:S(2)}) async-start(), calls=%async_computation.3 | async-start | bytes 524288 | tf_op jit(solution)/shard_map/psum | solution.py:22
  198.5 297.4 %all-reduce.8.cloned.1.call-start = ((), (), s32[]{:S(2)}) async-start(), calls=%async_computation.4 | async-start | bytes 524288 | tf_op jit(solution)/shard_map/psum | solution.py:22
  298.6 11.8 %collective-permute-start.4 = (f32[256,256]{0,1:T(8,128)S(1)}, f32[256,256]{0,1:T(8,128)S(1)}, u32[]{:S(2)}, u32[]{:S(2)}) collective-permute-start(f32[256,256]{0,1:T(8,128)S(1)} %collective-permute-done.3), channel_id=1, source_target_pairs={{0,8},{8,16},{16,24},{24,32},{32,40},{40,48},{48,56},{56,64},{64,7... | collective-permute-start | bytes 786440 | tf_op jit(solution)/shard_map/ppermute | solution.py:87
  298.7 12.0 %collective-permute-start.11 = (f32[256,256]{0,1:T(8,128)S(1)}, f32[256,256]{0,1:T(8,128)S(1)}, u32[]{:S(2)}, u32[]{:S(2)}) collective-permute-start(f32[256,256]{0,1:T(8,128)S(1)} %collective-permute-done.10), channel_id=1, source_target_pairs={{8,0},{16,8},{24,16},{32,24},{40,32},{48,40},{56,48},{64,56},{72,6... | collective-permute-start | bytes 786440 | tf_op jit(solution)/shard_map/ppermute | solution.py:90
  310.4 12.5 %collective-permute-start.5 = (f32[256,256]{0,1:T(8,128)S(1)}, f32[256,256]{0,1:T(8,128)}, u32[]{:S(2)}, u32[]{:S(2)}) collective-permute-start(f32[256,256]{0,1:T(8,128)S(1)} %collective-permute-done.4), channel_id=1, source_target_pairs={{0,8},{8,16},{16,24},{24,32},{32,40},{40,48},{48,56},{56,64},{64,7... | collective-permute-start | bytes 786440 | tf_op jit(solution)/shard_map/ppermute | solution.py:87
  310.7 12.2 %collective-permute-start.12 = (f32[256,256]{0,1:T(8,128)S(1)}, f32[256,256]{0,1:T(8,128)S(1)}, u32[]{:S(2)}, u32[]{:S(2)}) collective-permute-start(f32[256,256]{0,1:T(8,128)S(1)} %collective-permute-done.11), channel_id=1, source_target_pairs={{8,0},{16,8},{24,16},{32,24},{40,32},{48,40},{56,48},{64,56},{72,6... | collective-permute-start | bytes 786440 | tf_op jit(solution)/shard_map/ppermute | solution.py:90
  322.9 11.9 %collective-permute-start.6 = (f32[256,256]{0,1:T(8,128)}, f32[256,256]{0,1:T(8,128)}, u32[]{:S(2)}, u32[]{:S(2)}) collective-permute-start(f32[256,256]{0,1:T(8,128)} %collective-permute-done.5), channel_id=1, source_target_pairs={{0,8},{8,16},{16,24},{24,32},{32,40},{40,48},{48,56},{56,64},{64,7... | collective-permute-start | bytes 786440 | tf_op jit(solution)/shard_map/ppermute | solution.py:87
  322.9 12.6 %collective-permute-start.13 = (f32[256,256]{0,1:T(8,128)S(1)}, f32[256,256]{0,1:T(8,128)}, u32[]{:S(2)}, u32[]{:S(2)}) collective-permute-start(f32[256,256]{0,1:T(8,128)S(1)} %collective-permute-done.12), channel_id=1, source_target_pairs={{8,0},{16,8},{24,16},{32,24},{40,32},{48,40},{56,48},{64,56},{72,6... | collective-permute-start | bytes 786440 | tf_op jit(solution)/shard_map/ppermute | solution.py:90
  335.5 23.8 %collective-permute-start.14 = (f32[256,256]{0,1:T(8,128)}, f32[256,256]{0,1:T(8,128)S(1)}, u32[]{:S(2)}, u32[]{:S(2)}) collective-permute-start(f32[256,256]{0,1:T(8,128)} %collective-permute-done.13), channel_id=1, source_target_pairs={{8,0},{16,8},{24,16},{32,24},{40,32},{48,40},{56,48},{64,56},{72,6... | collective-permute-start | bytes 786440 | tf_op jit(solution)/shard_map/ppermute | solution.py:90
  442.0 290.4 %all-reduce.10.cloned.1.call-start = ((), (), s32[]{:S(2)}) async-start(), calls=%async_computation.5 | async-start | bytes 524288 | tf_op jit(solution)/shard_map/psum | solution.py:22
  535.8 11.8 %collective-permute-start.19 = (f32[256,256]{0,1:T(8,128)S(1)}, f32[256,256]{0,1:T(8,128)S(1)}, u32[]{:S(2)}, u32[]{:S(2)}) collective-permute-start(f32[256,256]{0,1:T(8,128)S(1)} %collective-permute-done.18), channel_id=1, source_target_pairs={{0,8},{8,16},{16,24},{24,32},{32,40},{40,48},{48,56},{56,64},{64,7... | collective-permute-start | bytes 786440 | tf_op jit(solution)/shard_map/ppermute | solution.py:87
  535.9 12.0 %collective-permute-start.26 = (f32[256,256]{0,1:T(8,128)S(1)}, f32[256,256]{0,1:T(8,128)S(1)}, u32[]{:S(2)}, u32[]{:S(2)}) collective-permute-start(f32[256,256]{0,1:T(8,128)S(1)} %collective-permute-done.25), channel_id=1, source_target_pairs={{8,0},{16,8},{24,16},{32,24},{40,32},{48,40},{56,48},{64,56},{72,6... | collective-permute-start | bytes 786440 | tf_op jit(solution)/shard_map/ppermute | solution.py:90
  547.6 12.1 %collective-permute-start.20 = (f32[256,256]{0,1:T(8,128)S(1)}, f32[256,256]{0,1:T(8,128)S(1)}, u32[]{:S(2)}, u32[]{:S(2)}) collective-permute-start(f32[256,256]{0,1:T(8,128)S(1)} %collective-permute-done.19), channel_id=1, source_target_pairs={{0,8},{8,16},{16,24},{24,32},{32,40},{40,48},{48,56},{56,64},{64,7... | collective-permute-start | bytes 786440 | tf_op jit(solution)/shard_map/ppermute | solution.py:87
  547.9 11.8 %collective-permute-start.27 = (f32[256,256]{0,1:T(8,128)S(1)}, f32[256,256]{0,1:T(8,128)S(1)}, u32[]{:S(2)}, u32[]{:S(2)}) collective-permute-start(f32[256,256]{0,1:T(8,128)S(1)} %collective-permute-done.26), channel_id=1, source_target_pairs={{8,0},{16,8},{24,16},{32,24},{40,32},{48,40},{56,48},{64,56},{72,6... | collective-permute-start | bytes 786440 | tf_op jit(solution)/shard_map/ppermute | solution.py:90
  559.7 11.5 collective-permute-start.21
  560.4 10.9 collective-permute-start.28
  571.3 24.5 %collective-permute-start.29 = (f32[256,256]{0,1:T(8,128)}, f32[256,256]{0,1:T(8,128)S(1)}, u32[]{:S(2)}, u32[]{:S(2)}) collective-permute-start(f32[256,256]{0,1:T(8,128)} %collective-permute-done.28), channel_id=1, source_target_pairs={{8,0},{16,8},{24,16},{32,24},{40,32},{48,40},{56,48},{64,56},{72,6... | collective-permute-start | bytes 786440 | tf_op jit(solution)/shard_map/ppermute | solution.py:90
  678.6 290.9 %all-reduce.12.cloned.1.call-start = ((), (), s32[]{:S(2)}) async-start(), calls=%async_computation.6 | async-start | bytes 524288 | tf_op jit(solution)/shard_map/psum | solution.py:22
  772.4 11.8 %collective-permute-start.34 = (f32[256,256]{0,1:T(8,128)S(1)}, f32[256,256]{0,1:T(8,128)S(1)}, u32[]{:S(2)}, u32[]{:S(2)}) collective-permute-start(f32[256,256]{0,1:T(8,128)S(1)} %collective-permute-done.33), channel_id=1, source_target_pairs={{0,8},{8,16},{16,24},{24,32},{32,40},{40,48},{48,56},{56,64},{64,7... | collective-permute-start | bytes 786440 | tf_op jit(solution)/shard_map/ppermute | solution.py:87
  772.5 12.0 %collective-permute-start.41 = (f32[256,256]{0,1:T(8,128)S(1)}, f32[256,256]{0,1:T(8,128)S(1)}, u32[]{:S(2)}, u32[]{:S(2)}) collective-permute-start(f32[256,256]{0,1:T(8,128)S(1)} %collective-permute-done.40), channel_id=1, source_target_pairs={{8,0},{16,8},{24,16},{32,24},{40,32},{48,40},{56,48},{64,56},{72,6... | collective-permute-start | bytes 786440 | tf_op jit(solution)/shard_map/ppermute | solution.py:90
  784.1 12.1 %collective-permute-start.35 = (f32[256,256]{0,1:T(8,128)S(1)}, f32[256,256]{0,1:T(8,128)S(1)}, u32[]{:S(2)}, u32[]{:S(2)}) collective-permute-start(f32[256,256]{0,1:T(8,128)S(1)} %collective-permute-done.34), channel_id=1, source_target_pairs={{0,8},{8,16},{16,24},{24,32},{32,40},{40,48},{48,56},{56,64},{64,7... | collective-permute-start | bytes 786440 | tf_op jit(solution)/shard_map/ppermute | solution.py:87
  784.5 11.8 %collective-permute-start.42 = (f32[256,256]{0,1:T(8,128)S(1)}, f32[256,256]{0,1:T(8,128)S(1)}, u32[]{:S(2)}, u32[]{:S(2)}) collective-permute-start(f32[256,256]{0,1:T(8,128)S(1)} %collective-permute-done.41), channel_id=1, source_target_pairs={{8,0},{16,8},{24,16},{32,24},{40,32},{48,40},{56,48},{64,56},{72,6... | collective-permute-start | bytes 786440 | tf_op jit(solution)/shard_map/ppermute | solution.py:90
  796.2 11.5 collective-permute-start.36
  807.8 24.5 %collective-permute-start.44 = (f32[256,256]{0,1:T(8,128)}, f32[256,256]{0,1:T(8,128)S(1)}, u32[]{:S(2)}, u32[]{:S(2)}) collective-permute-start(f32[256,256]{0,1:T(8,128)} %collective-permute-done.43), channel_id=1, source_target_pairs={{8,0},{16,8},{24,16},{32,24},{40,32},{48,40},{56,48},{64,56},{72,6... | collective-permute-start | bytes 786440 | tf_op jit(solution)/shard_map/ppermute | solution.py:90
  1009.4 11.8 %collective-permute-start.49 = (f32[256,256]{0,1:T(8,128)S(1)}, f32[256,256]{0,1:T(8,128)S(1)}, u32[]{:S(2)}, u32[]{:S(2)}) collective-permute-start(f32[256,256]{0,1:T(8,128)S(1)} %collective-permute-done.48), channel_id=1, source_target_pairs={{0,8},{8,16},{16,24},{24,32},{32,40},{40,48},{48,56},{56,64},{64,7... | collective-permute-start | bytes 786440 | tf_op jit(solution)/shard_map/ppermute | solution.py:87
  1009.5 12.0 %collective-permute-start.56 = (f32[256,256]{0,1:T(8,128)S(1)}, f32[256,256]{0,1:T(8,128)S(1)}, u32[]{:S(2)}, u32[]{:S(2)}) collective-permute-start(f32[256,256]{0,1:T(8,128)S(1)} %collective-permute-done.55), channel_id=1, source_target_pairs={{8,0},{16,8},{24,16},{32,24},{40,32},{48,40},{56,48},{64,56},{72,6... | collective-permute-start | bytes 786440 | tf_op jit(solution)/shard_map/ppermute | solution.py:90
  1021.2 12.1 %collective-permute-start.50 = (f32[256,256]{0,1:T(8,128)S(1)}, f32[256,256]{0,1:T(8,128)S(1)}, u32[]{:S(2)}, u32[]{:S(2)}) collective-permute-start(f32[256,256]{0,1:T(8,128)S(1)} %collective-permute-done.49), channel_id=1, source_target_pairs={{0,8},{8,16},{16,24},{24,32},{32,40},{40,48},{48,56},{56,64},{64,7... | collective-permute-start | bytes 786440 | tf_op jit(solution)/shard_map/ppermute | solution.py:87
  1021.5 11.8 %collective-permute-start.57 = (f32[256,256]{0,1:T(8,128)S(1)}, f32[256,256]{0,1:T(8,128)S(1)}, u32[]{:S(2)}, u32[]{:S(2)}) collective-permute-start(f32[256,256]{0,1:T(8,128)S(1)} %collective-permute-done.56), channel_id=1, source_target_pairs={{8,0},{16,8},{24,16},{32,24},{40,32},{48,40},{56,48},{64,56},{72,6... | collective-permute-start | bytes 786440 | tf_op jit(solution)/shard_map/ppermute | solution.py:90
  1033.3 11.2 collective-permute-start.51
  1033.4 11.4 collective-permute-start.58
  1044.7 20.2 %collective-permute-start.59 = (f32[256,256]{0,1:T(8,128)S(1)}, f32[256,256]{0,1:T(8,128)S(1)}, u32[]{:S(2)}, u32[]{:S(2)}) collective-permute-start(f32[256,256]{0,1:T(8,128)S(1)} %collective-permute-done.58), channel_id=1, source_target_pairs={{8,0},{16,8},{24,16},{32,24},{40,32},{48,40},{56,48},{64,56},{72,6... | collective-permute-start | bytes 786440 | tf_op jit(solution)/shard_map/ppermute | solution.py:90
  (41 other events, 707.4 us)
Sparse Core Ops, SparseCore 0:
  110.3 86.3 reduce-scatter.1
  199.0 59.6 all-reduce.5
  442.2 53.7 all-reduce.7
  678.7 53.7 all-reduce.9
  915.7 53.7 all-reduce.11
